TPU v7x, 32 devices: a whole 2x2x4 slice. The times are simulated.
32 devices in a mesh: groups: 2 (over x), freq: 16 (over z, y, core).
Axes of the slice: x: 2, y: 2, z: 4, core: 2. Of those that a mesh axis runs over, the one named last changes fastest.
Arguments:
- encoder_input: bfloat16 [64, 2048], P(('groups', 'freq')), parts along dimension 0, may hold values from -6 to 6
- desired_responses: bfloat16 [64, 384, 512], P('groups', 'freq'), parts along dimension 0, may hold values from -6 to 6
- sample_index: int32 [64], P('groups'), parts along dimension 0, may hold values from 0 to 31, each once
- encoder_weight: bfloat16 [2048, 512], replicated, may hold values from -0.125 to 0.125
- decoder_weight: bfloat16 [512, 512], replicated, may hold values from -0.25 to 0.25
- frequency_amplitude: bfloat16 [384, 512], P('freq'), may hold values from -4 to 4
- spectral_filter_weight: float32 [2, 256], replicated, may hold values from -4 to 4
- output_weight: bfloat16 [512, 512], replicated, may hold values from -0.25 to 0.25
Outputs:
- grad_enc: float32 [4096, 512], P('groups'), parts along dimension 0
- grad_dec: float32 [1024, 512], P('groups'), parts along dimension 0
- grad_out: float32 [1024, 512], P('groups'), parts along dimension 0
- grad_filter: float32 [4, 256], P('groups'), parts along dimension 0
There are 2 independent parts, one for each index of `groups`. A program takes and returns all parts, laid end to end along the dimension named above; an argument that names none is the same for every part. Nothing has to cross between parts.
Inputs may be any that keep to these rules, and one draw needn't show every extreme that they name: sample_index names each of the 32 samples once.
All inputs are finite; a program needn't handle non-finite values.
Results may differ from a plain program's by a relative error of at most 0.0065.
Values may be sent and summed in bfloat16 or wider, within the bound.
No kernel may reach another device: no remote copies, remote signals or barrier semaphores. Data moves between devices by JAX's collectives and lax.ppermute only.
A program may use at most 128 MiB of HBM per device.

v0:
```python
import math
import jax
import jax.numpy as jnp
from jax import lax
from jax.sharding import PartitionSpec as P


def rotation_tables(antennas):
    indices = jnp.arange(antennas, dtype=jnp.int32)
    products_mod = indices[:, None] * indices[None, :] % antennas
    angle_table = products_mod.astype(jnp.float32) * (2.0 * math.pi / antennas)
    cosine_table = jnp.cos(angle_table) / math.sqrt(antennas)
    sine_table = jnp.sin(angle_table) / math.sqrt(antennas)
    forward_transform = jnp.concatenate(
        [
            jnp.concatenate([cosine_table, -sine_table], 1),
            jnp.concatenate([sine_table, cosine_table], 1),
        ],
        0,
    )
    inverse_transform = jnp.concatenate(
        [
            jnp.concatenate([cosine_table, sine_table], 1),
            jnp.concatenate([-sine_table, cosine_table], 1),
        ],
        0,
    )
    return (forward_transform.astype(jnp.bfloat16), inverse_transform.astype(jnp.bfloat16))


def decode_rows(
    mixed_in,
    wanted_lines,
    output_weight,
    spectral_filter_weight,
    forward_transform,
    inverse_transform,
    loss_scale,
):
    filter_re = spectral_filter_weight[0]
    filter_im = spectral_filter_weight[1]
    spectrum = jnp.dot(mixed_in, forward_transform, preferred_element_type=jnp.float32)
    half_width = spectrum.shape[1] // 2
    spec_re = spectrum[:, :half_width]
    spec_im = spectrum[:, half_width:]
    filtered = jnp.concatenate(
        [spec_re * filter_re - spec_im * filter_im, spec_re * filter_im + spec_im * filter_re], 1
    ).astype(jnp.bfloat16)
    mixed_back = jnp.dot(filtered, inverse_transform, preferred_element_type=jnp.float32)
    hidden = (mixed_in.astype(jnp.float32) + jax.nn.gelu(mixed_back)).astype(jnp.bfloat16)
    rebuilt = hidden.astype(jnp.float32) + jnp.dot(
        hidden, output_weight, preferred_element_type=jnp.float32
    )
    residual = loss_scale * (rebuilt - wanted_lines.astype(jnp.float32))
    residual_half = residual.astype(jnp.bfloat16)
    grad_out = lax.dot_general(
        hidden, residual_half, (((0,), (0,)), ((), ())), preferred_element_type=jnp.float32
    )
    grad_hidden = residual + lax.dot_general(
        residual_half, output_weight, (((1,), (1,)), ((), ())), preferred_element_type=jnp.float32
    )
    grad_mixed = jax.vjp(jax.nn.gelu, mixed_back)[1](grad_hidden)[0].astype(jnp.bfloat16)
    grad_filtered = lax.dot_general(
        grad_mixed, inverse_transform, (((1,), (1,)), ((), ())), preferred_element_type=jnp.float32
    )
    grad_re = grad_filtered[:, :half_width]
    grad_im = grad_filtered[:, half_width:]
    grad_filter = jnp.stack(
        [
            jnp.sum(grad_re * spec_re + grad_im * spec_im, 0),
            jnp.sum(grad_im * spec_re - grad_re * spec_im, 0),
        ]
    )
    grad_spec = jnp.concatenate(
        [grad_re * filter_re + grad_im * filter_im, grad_im * filter_re - grad_re * filter_im], 1
    ).astype(jnp.bfloat16)
    derivative_entering = grad_hidden + lax.dot_general(
        grad_spec, forward_transform, (((1,), (1,)), ((), ())), preferred_element_type=jnp.float32
    )
    return (derivative_entering, grad_out, grad_filter)


def encoder_grads(inputs_rows, codewords, latent_sums, decoder_weight):
    latent_half = latent_sums.astype(jnp.bfloat16)
    grad_dec = lax.dot_general(
        codewords, latent_half, (((0,), (0,)), ((), ())), preferred_element_type=jnp.float32
    )
    grad_codes = lax.dot_general(
        latent_half, decoder_weight, (((1,), (1,)), ((), ())), preferred_element_type=jnp.float32
    )
    grad_pre = (grad_codes * (1.0 - jnp.square(codewords.astype(jnp.float32)))).astype(jnp.bfloat16)
    grad_enc = lax.dot_general(
        inputs_rows, grad_pre, (((0,), (0,)), ((), ())), preferred_element_type=jnp.float32
    )
    return (grad_enc, grad_dec)


def local(
    encoder_input,
    desired_responses,
    sample_index,
    encoder_weight,
    decoder_weight,
    frequency_amplitude,
    spectral_filter_weight,
    output_weight,
):
    samples = sample_index.shape[0]
    sub_dev = desired_responses.shape[1]
    width = desired_responses.shape[2]
    forward_transform, inverse_transform = rotation_tables(width // 2)
    loss_scale = 1.0 / math.sqrt(samples * sub_dev * lax.axis_size("freq"))
    codes_own = jnp.tanh(
        jnp.dot(encoder_input, encoder_weight, preferred_element_type=jnp.float32)
    ).astype(jnp.bfloat16)
    all_codes = lax.all_gather(codes_own, "freq", axis=0, tiled=True)
    inverse_ids = (
        jnp.zeros((samples,), jnp.int32).at[sample_index].set(jnp.arange(samples, dtype=jnp.int32))
    )
    latent = jnp.dot(all_codes[inverse_ids], decoder_weight, preferred_element_type=jnp.float32)
    gain_row_values = frequency_amplitude.astype(jnp.float32)
    mixed_in = (latent[:, None, :] * gain_row_values[None]).astype(jnp.bfloat16).reshape(-1, width)
    wanted_lines = desired_responses.reshape(-1, width)
    derivative_entering, grad_out, grad_filter = decode_rows(
        mixed_in,
        wanted_lines,
        output_weight,
        spectral_filter_weight,
        forward_transform,
        inverse_transform,
        loss_scale,
    )
    derivative_bottleneck = jnp.einsum(
        "orm,rm->om", derivative_entering.reshape(samples, sub_dev, width), gain_row_values
    )
    enc_order = derivative_bottleneck[sample_index]
    owned_rows = lax.psum_scatter(enc_order, "freq", scatter_dimension=0, tiled=True)
    grad_enc, grad_dec = encoder_grads(encoder_input, codes_own, owned_rows, decoder_weight)
    grad_enc, grad_dec, grad_out, grad_filter = lax.psum(
        (grad_enc, grad_dec, grad_out, grad_filter), "freq"
    )
    return (grad_enc, grad_dec, grad_out, grad_filter)


def solution(mesh):
    return jax.shard_map(
        local,
        mesh=mesh,
        in_specs=(
            P(("groups", "freq"), None),
            P("groups", "freq", None),
            P("groups"),
            P(),
            P(),
            P("freq", None),
            P(),
            P(),
        ),
        out_specs=(P("groups", None), P("groups", None), P("groups", None), P("groups", None)),
        check_vma=False,
    )
```

profile of v0, /device:TPU:0, one launch (start us, length us, event | category | flops | bytes accessed | tf_op | source)
XLA Modules:
  0.0 264.4 jit_solution(11074158935546057527)
XLA Ops:
  7.3 1.0 fusion.30
  8.3 1.1 negate_convert_fusion
  9.4 0.7 compare_select_fusion.1
  10.1 0.7 scatter_custom_fusion
  10.8 0.8 fusion.54
  11.6 1.1 fusion.8
  12.7 23.2 %all-gather = bf16[16,2,512]{2,1,0:T(2,128)(2,1)S(1)} all-gather(bf16[1,2,512]{2,1,0:T(2,128)(2,1)S(1)} %bitcast.34), channel_id=1, replica_groups=mesh['groups'=2,'freq'=16] {'freq'}, dimensions={0}, use_global_device_ids=true | all-gather | bytes 34816 | tf_op jit(solution)/shard_map/all_gather | solution.py:116
  35.9 0.6 gather_fusion
  36.9 0.6 fusion.34
  37.7 1.0 add_convert_fusion
  39.0 0.6 fusion.7
  39.6 1.6 fusion.21
  41.2 0.6 convolution_add_fusion.1
  41.8 1.2 fusion.17
  43.7 0.6 dynamic-slice
  45.0 2.3 convolution_add_fusion
  47.6 0.6 gather_fusion.1
  48.2 59.2 %all-reduce.1 = (bf16[32,512]{1,0:T(8,128)(2,1)S(1)}, f32[2,256]{1,0:T(2,128)}) all-reduce(f32[32,512]{1,0:T(8,128)S(1)} %gather_fusion.1, f32[2,256]{1,0:T(2,128)S(1)} %pad_maximum_fusion.4), channel_id=2, replica_groups=mesh['groups'=2,'freq'=16] {'freq'}, use_global_device_ids=true, to_apply=%region_1.2.clone | all-reduce | flops 16896 | bytes 102400
  107.4 1.3 fusion.53
  108.7 3.0 %convolution_bitcast_fusion = f32[2048,512]{0,1:T(8,128)} fusion(bf16[2,2048]{1,0:T(2,128)(2,1)S(1)} %copy-done.8, bf16[512,512]{1,0:T(8,128)(2,1)S(1)} %copy-done.1, bf16[2,512]{1,0:T(2,128)(2,1)S(1)} %fusion.8, bf16[32,512]{1,0:T(8,128)(2,1)S(1)} %get-tuple-element.14, u32[]{:T(128)S(6)} %multiply.6), kind=kOutput, calls=%fused_computation.3 | convolution fusion | flops 5248000 | bytes 4730884 | tf_op jit(solution)/shard_map/dot_general | solution.py:92
  111.8 137.2 %all-reduce.5.cloned.1.call-done = (f32[2048,512]{0,1:T(8,128)}, f32[512,512]{1,0:T(8,128)}, f32[512,512]{1,0:T(8,128)}) async-done(((f32[2048,512]{0,1:T(8,128)}, f32[512,512]{1,0:T(8,128)}, f32[512,512]{1,0:T(8,128)}), (f32[2048,512]{0,1:T(8,128)}, f32[512,512]{1,0:T(8,128)}, f32[512,512]{1,0:T(8,128)})) %all-reduce.5.cloned.1.call-update) | async-done | bytes 6291472 | tf_op jit(solution)/shard_map/psum | solution.py:139
  248.9 5.3 %copy.13 = f32[2048,512]{1,0:T(8,128)} copy(f32[2048,512]{0,1:T(8,128)} %get-tuple-element.16) | data formatting | bytes 8388608
  254.3 2.4 copy.25
  256.6 1.0 copy.26
  (38 shorter events, 2.0 us)
Async XLA Ops:
  7.2 4.4 %copy-start = (bf16[2048,512]{1,0:T(8,128)(2,1)S(1)}, bf16[2048,512]{1,0:T(8,128)(2,1)}, u32[]{:S(2)}) copy-start(bf16[2048,512]{1,0:T(8,128)(2,1)} %param.11) | copy-start | bytes 6291460
  7.2 28.7 %copy-start.9 = (bf16[24,512]{1,0:T(8,128)(2,1)S(1)}, bf16[24,512]{1,0:T(8,128)(2,1)}, u32[]{:S(2)}) copy-start(bf16[24,512]{1,0:T(8,128)(2,1)} %param.13) | copy-start | bytes 73732
  7.2 29.3 %copy-start.1 = (bf16[512,512]{1,0:T(8,128)(2,1)S(1)}, bf16[512,512]{1,0:T(8,128)(2,1)}, u32[]{:S(2)}) copy-start(bf16[512,512]{1,0:T(8,128)(2,1)} %param.12) | copy-start | bytes 1572868
  7.2 241.7 %all-reduce.5.cloned.1.call-start = ((), (), s32[]{:S(2)}) async-start(), calls=%async_computation | async-start | bytes 12582912 | tf_op jit(solution)/shard_map/psum | solution.py:139
  8.3 33.6 %copy-start.5 = (bf16[256,256]{1,0:T(8,128)(2,1)}, bf16[256,256]{1,0:T(8,128)(2,1)S(1)}, u32[]{:S(2)}) copy-start(bf16[256,256]{1,0:T(8,128)(2,1)S(1)} %fusion.30) | copy-start | bytes 393220
  9.4 32.4 %copy-start.6 = (bf16[256,256]{1,0:T(8,128)(2,1)}, bf16[256,256]{1,0:T(8,128)(2,1)S(1)}, u32[]{:S(2)}) copy-start(bf16[256,256]{1,0:T(8,128)(2,1)S(1)} %get-tuple-element.31) | copy-start | bytes 393220
  9.4 32.4 %copy-start.7 = (bf16[256,256]{1,0:T(8,128)(2,1)}, bf16[256,256]{1,0:T(8,128)(2,1)S(1)}, u32[]{:S(2)}) copy-start(bf16[256,256]{1,0:T(8,128)(2,1)S(1)} %get-tuple-element.32) | copy-start | bytes 393220
  37.7 1.0 copy-start.4
  37.7 1.3 copy-start.10
  41.8 1.3 copy-start.2
  43.1 0.7 copy-start.11
  47.2 61.5 %copy-start.8 = (bf16[2,2048]{1,0:T(2,128)(2,1)S(1)}, bf16[2,2048]{1,0:T(2,128)(2,1)}, u32[]{:S(2)}) copy-start(bf16[2,2048]{1,0:T(2,128)(2,1)} %param.8) | copy-start | bytes 24580
  254.3 2.4 copy-start.3
Sparse Core Ops, SparseCore 0:
  111.9 136.9 all-reduce.4
where the time goes:
time: 265 us; the launch traced here: 264 us
  waiting for transfers between devices  137 us (52%)
  blocking collectives  82.4 us (31%)
  between operations  14.9 us (6%)
  matrix products  13.4 us (5%)
  local copies, waits for them, and re-layouts  12.5 us (5%)
  other arithmetic  3.97 us (1%)
    psum x1, waiting for transfers between devices, local(): lax.psum((grad_enc, grad_dec, grad_out, grad_filter), 'freq')  137 us
    unnamed x1, blocking collectives  59.2 us
    all_gather x1, blocking collectives, local(): all_codes = lax.all_gather(codes_own, 'freq', axis=0, tiled=True)  23.2 us
    unnamed x29, local copies, waits for them, and re-layouts  9.8 us
  transfers between devices with their start and end apart: 1, of which 1 were waited for; matrix products, arithmetic and copies ran while one was open for 0% of the time, Pallas kernels for 0%

commit v1 on v0

--- a/solution.py
+++ b/solution.py
@@ -1,8 +1,27 @@
+import functools
 import math
 import jax
 import jax.numpy as jnp
 from jax import lax
 from jax.sharding import PartitionSpec as P
+
+
+def point_body(target, at_axis):
+    axis_len = lax.psum(1, "freq")
+    carry = sorted(((i, (i + 1) % axis_len) for i in range(axis_len)))
+    w1 = target
+    by_place = [w1]
+    for hop_no in range(1, axis_len):
+        w1 = lax.ppermute(w1, "freq", carry)
+        by_place.insert(0, w1)
+    return jnp.roll(
+        jnp.concatenate(by_place, at_axis),
+        (lax.axis_index("freq") + 1) * target.shape[at_axis],
+        at_axis,
+    )
+
+
+_write_seats_all = functools.partial(point_body, at_axis=0)
 
 
 def rotation_tables(antennas):
@@ -113,7 +132,7 @@
     codes_own = jnp.tanh(
         jnp.dot(encoder_input, encoder_weight, preferred_element_type=jnp.float32)
     ).astype(jnp.bfloat16)
-    all_codes = lax.all_gather(codes_own, "freq", axis=0, tiled=True)
+    all_codes = _write_seats_all(codes_own)
     inverse_ids = (
         jnp.zeros((samples,), jnp.int32).at[sample_index].set(jnp.arange(samples, dtype=jnp.int32))
     )

time: 265 us -> 322 us (1.22)
  waiting for transfers between devices: 137 us -> 220 us
  blocking collectives: 82.4 us -> 58.9 us
    ppermute x0 -> x15, waiting for transfers between devices: none -> 82 us  [point_body(): w1 = lax.ppermute(w1, 'freq', carry)]
    all_gather x1 -> x0, blocking collectives: 23.2 us -> none  [local(): all_codes = lax.all_gather(codes_own, 'freq', axis=0, tiled=True)]
    unnamed x29 -> x26, local copies, waits for them, and re-layouts: 9.8 us -> 10.4 us
  transfers between devices with their start and end apart: 1 -> 16, of which waited for: 1 -> 16; matrix products, arithmetic and copies ran while one was open for 0% -> 1% of each run, Pallas kernels for 0% -> 0%
where the time goes in v1:
time: 322 us
  waiting for transfers between devices  220 us (68%)
  blocking collectives  58.9 us (18%)
  between operations  14.9 us (5%)
  local copies, waits for them, and re-layouts  12.6 us (4%)
  matrix products  11.8 us (4%)
  other arithmetic  3.26 us (1%)
    psum x1, waiting for transfers between devices, local(): lax.psum((grad_enc, grad_dec, grad_out, grad_filter), 'freq')  138 us
    ppermute x15, waiting for transfers between devices, point_body(): w1 = lax.ppermute(w1, 'freq', carry)  82 us
    unnamed x1, blocking collectives  58.9 us
    unnamed x26, local copies, waits for them, and re-layouts  10.4 us
  transfers between devices with their start and end apart: 16, of which 16 were waited for; matrix products, arithmetic and copies ran while one was open for 1% of the time, Pallas kernels for 0%

profile of v1, /device:TPU:0, one launch (start us, length us, event | category | flops | bytes accessed | tf_op | source)
XLA Modules:
  0.0 321.7 jit_solution(14742233222984866315)
XLA Ops:
  7.3 1.5 copy-done
  10.3 6.3 %collective-permute-done = bf16[2,512]{1,0:T(2,128)(2,1)S(1)} collective-permute-done((bf16[2,512]{1,0:T(2,128)(2,1)S(1)}, bf16[2,512]{1,0:T(2,128)(2,1)S(1)}, u32[]{:S(2)}, u32[]{:S(2)}) %collective-permute-start) | collective-permute-done | bytes 2080 | tf_op jit(solution)/shard_map/ppermute | solution.py:15
  16.6 5.7 %collective-permute-done.1 = bf16[2,512]{1,0:T(2,128)(2,1)S(1)} collective-permute-done((bf16[2,512]{1,0:T(2,128)(2,1)S(1)}, bf16[2,512]{1,0:T(2,128)(2,1)S(1)}, u32[]{:S(2)}, u32[]{:S(2)}) %collective-permute-start.1) | collective-permute-done | bytes 2080 | tf_op jit(solution)/shard_map/ppermute | solution.py:15
  22.3 5.7 %collective-permute-done.2 = bf16[2,512]{1,0:T(2,128)(2,1)S(1)} collective-permute-done((bf16[2,512]{1,0:T(2,128)(2,1)S(1)}, bf16[2,512]{1,0:T(2,128)(2,1)S(1)}, u32[]{:S(2)}, u32[]{:S(2)}) %collective-permute-start.2) | collective-permute-done | bytes 2080 | tf_op jit(solution)/shard_map/ppermute | solution.py:15
  28.0 5.7 %collective-permute-done.3 = bf16[2,512]{1,0:T(2,128)(2,1)S(1)} collective-permute-done((bf16[2,512]{1,0:T(2,128)(2,1)S(1)}, bf16[2,512]{1,0:T(2,128)(2,1)S(1)}, u32[]{:S(2)}, u32[]{:S(2)}) %collective-permute-start.3) | collective-permute-done | bytes 2080 | tf_op jit(solution)/shard_map/ppermute | solution.py:15
  33.7 5.7 %collective-permute-done.4 = bf16[2,512]{1,0:T(2,128)(2,1)S(1)} collective-permute-done((bf16[2,512]{1,0:T(2,128)(2,1)S(1)}, bf16[2,512]{1,0:T(2,128)(2,1)S(1)}, u32[]{:S(2)}, u32[]{:S(2)}) %collective-permute-start.4) | collective-permute-done | bytes 2080 | tf_op jit(solution)/shard_map/ppermute | solution.py:15
  39.4 5.7 %collective-permute-done.5 = bf16[2,512]{1,0:T(2,128)(2,1)S(1)} collective-permute-done((bf16[2,512]{1,0:T(2,128)(2,1)S(1)}, bf16[2,512]{1,0:T(2,128)(2,1)S(1)}, u32[]{:S(2)}, u32[]{:S(2)}) %collective-permute-start.5) | collective-permute-done | bytes 2080 | tf_op jit(solution)/shard_map/ppermute | solution.py:15
  45.1 5.7 %collective-permute-done.6 = bf16[2,512]{1,0:T(2,128)(2,1)S(1)} collective-permute-done((bf16[2,512]{1,0:T(2,128)(2,1)S(1)}, bf16[2,512]{1,0:T(2,128)(2,1)S(1)}, u32[]{:S(2)}, u32[]{:S(2)}) %collective-permute-start.6) | collective-permute-done | bytes 2080 | tf_op jit(solution)/shard_map/ppermute | solution.py:15
  50.9 5.7 %collective-permute-done.7 = bf16[2,512]{1,0:T(2,128)(2,1)S(1)} collective-permute-done((bf16[2,512]{1,0:T(2,128)(2,1)S(1)}, bf16[2,512]{1,0:T(2,128)(2,1)S(1)}, u32[]{:S(2)}, u32[]{:S(2)}) %collective-permute-start.7) | collective-permute-done | bytes 2080 | tf_op jit(solution)/shard_map/ppermute | solution.py:15
  56.6 5.7 %collective-permute-done.8 = bf16[2,512]{1,0:T(2,128)(2,1)S(1)} collective-permute-done((bf16[2,512]{1,0:T(2,128)(2,1)S(1)}, bf16[2,512]{1,0:T(2,128)(2,1)S(1)}, u32[]{:S(2)}, u32[]{:S(2)}) %collective-permute-start.8) | collective-permute-done | bytes 2080 | tf_op jit(solution)/shard_map/ppermute | solution.py:15
  63.0 5.0 %collective-permute-done.9 = bf16[2,512]{1,0:T(2,128)(2,1)S(1)} collective-permute-done((bf16[2,512]{1,0:T(2,128)(2,1)S(1)}, bf16[2,512]{1,0:T(2,128)(2,1)S(1)}, u32[]{:S(2)}, u32[]{:S(2)}) %collective-permute-start.9) | collective-permute-done | bytes 2080 | tf_op jit(solution)/shard_map/ppermute | solution.py:15
  68.0 5.7 %collective-permute-done.10 = bf16[2,512]{1,0:T(2,128)(2,1)S(1)} collective-permute-done((bf16[2,512]{1,0:T(2,128)(2,1)S(1)}, bf16[2,512]{1,0:T(2,128)(2,1)S(1)}, u32[]{:S(2)}, u32[]{:S(2)}) %collective-permute-start.10) | collective-permute-done | bytes 2080 | tf_op jit(solution)/shard_map/ppermute | solution.py:15
  73.7 1.1 negate_convert_fusion
  74.8 4.6 %collective-permute-done.11 = bf16[2,512]{1,0:T(2,128)(2,1)S(1)} collective-permute-done((bf16[2,512]{1,0:T(2,128)(2,1)S(1)}, bf16[2,512]{1,0:T(2,128)(2,1)S(1)}, u32[]{:S(2)}, u32[]{:S(2)}) %collective-permute-start.11) | collective-permute-done | bytes 2080 | tf_op jit(solution)/shard_map/ppermute | solution.py:15
  80.4 4.7 %collective-permute-done.12 = bf16[2,512]{1,0:T(2,128)(2,1)S(1)} collective-permute-done((bf16[2,512]{1,0:T(2,128)(2,1)S(1)}, bf16[2,512]{1,0:T(2,128)(2,1)S(1)}, u32[]{:S(2)}, u32[]{:S(2)}) %collective-permute-start.12) | collective-permute-done | bytes 2080 | tf_op jit(solution)/shard_map/ppermute | solution.py:15
  85.1 5.7 %collective-permute-done.13 = bf16[2,512]{1,0:T(2,128)(2,1)S(1)} collective-permute-done((bf16[2,512]{1,0:T(2,128)(2,1)S(1)}, bf16[2,512]{1,0:T(2,128)(2,1)S(1)}, u32[]{:S(2)}, u32[]{:S(2)}) %collective-permute-start.13) | collective-permute-done | bytes 2080 | tf_op jit(solution)/shard_map/ppermute | solution.py:15
  92.1 4.4 %collective-permute-done.14 = bf16[2,512]{1,0:T(2,128)(2,1)S(1)} collective-permute-done((bf16[2,512]{1,0:T(2,128)(2,1)S(1)}, bf16[2,512]{1,0:T(2,128)(2,1)S(1)}, u32[]{:S(2)}, u32[]{:S(2)}) %collective-permute-start.14) | collective-permute-done | bytes 2080 | tf_op jit(solution)/shard_map/ppermute | solution.py:15
  100.5 1.6 fusion.21
  102.7 1.2 fusion.17
  105.9 58.9 %all-reduce.1 = (bf16[32,512]{1,0:T(8,128)(2,1)S(1)}, f32[2,256]{1,0:T(2,128)}) all-reduce(f32[32,512]{1,0:T(8,128)S(1)} %gather_fusion.1, f32[2,256]{1,0:T(2,128)S(1)} %pad_maximum_fusion.4), channel_id=2, replica_groups=mesh['groups'=2,'freq'=16] {'freq'}, use_global_device_ids=true, to_apply=%region_1.2.clone | all-reduce | flops 16896 | bytes 102400
  164.9 1.3 fusion.53
  166.2 3.0 convolution_bitcast_fusion
  169.2 137.6 %all-reduce.5.cloned.1.call-done = (f32[2048,512]{0,1:T(8,128)}, f32[512,512]{1,0:T(8,128)}, f32[512,512]{1,0:T(8,128)}) async-done(((f32[2048,512]{0,1:T(8,128)}, f32[512,512]{1,0:T(8,128)}, f32[512,512]{1,0:T(8,128)}), (f32[2048,512]{0,1:T(8,128)}, f32[512,512]{1,0:T(8,128)}, f32[512,512]{1,0:T(8,128)})) %all-reduce.5.cloned.1.call-update) | async-done | bytes 6291472 | tf_op jit(solution)/shard_map/psum | solution.py:158
  306.8 5.4 %copy.13 = f32[2048,512]{1,0:T(8,128)} copy(f32[2048,512]{0,1:T(8,128)} %get-tuple-element.16) | data formatting | bytes 8388608
  (66 shorter events, 13.0 us)
Async XLA Ops:
  7.2 1.6 copy-start
  7.2 83.6 %copy-start.10 = (u32[32]{0:T(128)S(1)}, u32[32]{0:T(128)}, u32[]{:S(2)}) copy-start(u32[32]{0:T(128)} %constant.75) | copy-start | bytes 388
  7.2 43.7 %copy-start.6 = (bf16[24,512]{1,0:T(8,128)(2,1)S(1)}, bf16[24,512]{1,0:T(8,128)(2,1)}, u32[]{:S(2)}) copy-start(bf16[24,512]{1,0:T(8,128)(2,1)} %param.13) | copy-start | bytes 73732
  7.2 49.3 %copy-start.7 = (f32[2,256]{1,0:T(2,128)S(1)}, f32[2,256]{1,0:T(2,128)}, u32[]{:S(2)}) copy-start(f32[2,256]{1,0:T(2,128)} %param.14) | copy-start | bytes 6148
  7.2 55.0 %copy-start.9 = (s32[32]{0:T(128)S(1)}, s32[32]{0:T(128)}, u32[]{:S(2)}) copy-start(s32[32]{0:T(128)} %param.10) | copy-start | bytes 388
  7.2 90.2 %copy-start.1 = (bf16[512,512]{1,0:T(8,128)(2,1)S(1)}, bf16[512,512]{1,0:T(8,128)(2,1)}, u32[]{:S(2)}) copy-start(bf16[512,512]{1,0:T(8,128)(2,1)} %param.12) | copy-start | bytes 1572868
  7.2 299.6 %all-reduce.5.cloned.1.call-start = ((), (), s32[]{:S(2)}) async-start(), calls=%async_computation | async-start | bytes 12582912 | tf_op jit(solution)/shard_map/psum | solution.py:158
  9.9 6.7 %collective-permute-start = (bf16[2,512]{1,0:T(2,128)(2,1)S(1)}, bf16[2,512]{1,0:T(2,128)(2,1)S(1)}, u32[]{:S(2)}, u32[]{:S(2)}) collective-permute-start(bf16[2,512]{1,0:T(2,128)(2,1)S(1)} %fusion.8), channel_id=1, source_target_pairs={{0,1},{1,2},{2,3},{3,4},{4,5},{5,6},{6,7},{7,8},{8,9},{9,10},{10,1... | collective-permute-start | bytes 6152 | tf_op jit(solution)/shard_map/ppermute | solution.py:15
  16.6 5.7 %collective-permute-start.1 = (bf16[2,512]{1,0:T(2,128)(2,1)S(1)}, bf16[2,512]{1,0:T(2,128)(2,1)S(1)}, u32[]{:S(2)}, u32[]{:S(2)}) collective-permute-start(bf16[2,512]{1,0:T(2,128)(2,1)S(1)} %collective-permute-done), channel_id=1, source_target_pairs={{0,1},{1,2},{2,3},{3,4},{4,5},{5,6},{6,7},{7,8},{8,9},{9,10},{10,1... | collective-permute-start | bytes 6152 | tf_op jit(solution)/shard_map/ppermute | solution.py:15
  22.3 5.7 %collective-permute-start.2 = (bf16[2,512]{1,0:T(2,128)(2,1)S(1)}, bf16[2,512]{1,0:T(2,128)(2,1)S(1)}, u32[]{:S(2)}, u32[]{:S(2)}) collective-permute-start(bf16[2,512]{1,0:T(2,128)(2,1)S(1)} %collective-permute-done.1), channel_id=1, source_target_pairs={{0,1},{1,2},{2,3},{3,4},{4,5},{5,6},{6,7},{7,8},{8,9},{9,10},{10,1... | collective-permute-start | bytes 6152 | tf_op jit(solution)/shard_map/ppermute | solution.py:15
  28.0 5.7 %collective-permute-start.3 = (bf16[2,512]{1,0:T(2,128)(2,1)S(1)}, bf16[2,512]{1,0:T(2,128)(2,1)S(1)}, u32[]{:S(2)}, u32[]{:S(2)}) collective-permute-start(bf16[2,512]{1,0:T(2,128)(2,1)S(1)} %collective-permute-done.2), channel_id=1, source_target_pairs={{0,1},{1,2},{2,3},{3,4},{4,5},{5,6},{6,7},{7,8},{8,9},{9,10},{10,1... | collective-permute-start | bytes 6152 | tf_op jit(solution)/shard_map/ppermute | solution.py:15
  33.7 5.7 %collective-permute-start.4 = (bf16[2,512]{1,0:T(2,128)(2,1)S(1)}, bf16[2,512]{1,0:T(2,128)(2,1)S(1)}, u32[]{:S(2)}, u32[]{:S(2)}) collective-permute-start(bf16[2,512]{1,0:T(2,128)(2,1)S(1)} %collective-permute-done.3), channel_id=1, source_target_pairs={{0,1},{1,2},{2,3},{3,4},{4,5},{5,6},{6,7},{7,8},{8,9},{9,10},{10,1... | collective-permute-start | bytes 6152 | tf_op jit(solution)/shard_map/ppermute | solution.py:15
  39.4 5.7 %collective-permute-start.5 = (bf16[2,512]{1,0:T(2,128)(2,1)S(1)}, bf16[2,512]{1,0:T(2,128)(2,1)S(1)}, u32[]{:S(2)}, u32[]{:S(2)}) collective-permute-start(bf16[2,512]{1,0:T(2,128)(2,1)S(1)} %collective-permute-done.4), channel_id=1, source_target_pairs={{0,1},{1,2},{2,3},{3,4},{4,5},{5,6},{6,7},{7,8},{8,9},{9,10},{10,1... | collective-permute-start | bytes 6152 | tf_op jit(solution)/shard_map/ppermute | solution.py:15
  45.1 5.7 %collective-permute-start.6 = (bf16[2,512]{1,0:T(2,128)(2,1)S(1)}, bf16[2,512]{1,0:T(2,128)(2,1)S(1)}, u32[]{:S(2)}, u32[]{:S(2)}) collective-permute-start(bf16[2,512]{1,0:T(2,128)(2,1)S(1)} %collective-permute-done.5), channel_id=1, source_target_pairs={{0,1},{1,2},{2,3},{3,4},{4,5},{5,6},{6,7},{7,8},{8,9},{9,10},{10,1... | collective-permute-start | bytes 6152 | tf_op jit(solution)/shard_map/ppermute | solution.py:15
  50.8 5.7 %collective-permute-start.7 = (bf16[2,512]{1,0:T(2,128)(2,1)S(1)}, bf16[2,512]{1,0:T(2,128)(2,1)S(1)}, u32[]{:S(2)}, u32[]{:S(2)}) collective-permute-start(bf16[2,512]{1,0:T(2,128)(2,1)S(1)} %collective-permute-done.6), channel_id=1, source_target_pairs={{0,1},{1,2},{2,3},{3,4},{4,5},{5,6},{6,7},{7,8},{8,9},{9,10},{10,1... | collective-permute-start | bytes 6152 | tf_op jit(solution)/shard_map/ppermute | solution.py:15
  56.5 5.7 %collective-permute-start.8 = (bf16[2,512]{1,0:T(2,128)(2,1)S(1)}, bf16[2,512]{1,0:T(2,128)(2,1)S(1)}, u32[]{:S(2)}, u32[]{:S(2)}) collective-permute-start(bf16[2,512]{1,0:T(2,128)(2,1)S(1)} %collective-permute-done.7), channel_id=1, source_target_pairs={{0,1},{1,2},{2,3},{3,4},{4,5},{5,6},{6,7},{7,8},{8,9},{9,10},{10,1... | collective-permute-start | bytes 6152 | tf_op jit(solution)/shard_map/ppermute | solution.py:15
  62.3 5.7 %collective-permute-start.9 = (bf16[2,512]{1,0:T(2,128)(2,1)S(1)}, bf16[2,512]{1,0:T(2,128)(2,1)S(1)}, u32[]{:S(2)}, u32[]{:S(2)}) collective-permute-start(bf16[2,512]{1,0:T(2,128)(2,1)S(1)} %collective-permute-done.8), channel_id=1, source_target_pairs={{0,1},{1,2},{2,3},{3,4},{4,5},{5,6},{6,7},{7,8},{8,9},{9,10},{10,1... | collective-permute-start | bytes 6152 | tf_op jit(solution)/shard_map/ppermute | solution.py:15
  68.0 5.7 %collective-permute-start.10 = (bf16[2,512]{1,0:T(2,128)(2,1)S(1)}, bf16[2,512]{1,0:T(2,128)(2,1)S(1)}, u32[]{:S(2)}, u32[]{:S(2)}) collective-permute-start(bf16[2,512]{1,0:T(2,128)(2,1)S(1)} %collective-permute-done.9), channel_id=1, source_target_pairs={{0,1},{1,2},{2,3},{3,4},{4,5},{5,6},{6,7},{7,8},{8,9},{9,10},{10,1... | collective-permute-start | bytes 6152 | tf_op jit(solution)/shard_map/ppermute | solution.py:15
  73.7 5.7 %collective-permute-start.11 = (bf16[2,512]{1,0:T(2,128)(2,1)S(1)}, bf16[2,512]{1,0:T(2,128)(2,1)S(1)}, u32[]{:S(2)}, u32[]{:S(2)}) collective-permute-start(bf16[2,512]{1,0:T(2,128)(2,1)S(1)} %collective-permute-done.10), channel_id=1, source_target_pairs={{0,1},{1,2},{2,3},{3,4},{4,5},{5,6},{6,7},{7,8},{8,9},{9,10},{10,1... | collective-permute-start | bytes 6152 | tf_op jit(solution)/shard_map/ppermute | solution.py:15
  79.4 5.7 %collective-permute-start.12 = (bf16[2,512]{1,0:T(2,128)(2,1)S(1)}, bf16[2,512]{1,0:T(2,128)(2,1)S(1)}, u32[]{:S(2)}, u32[]{:S(2)}) collective-permute-start(bf16[2,512]{1,0:T(2,128)(2,1)S(1)} %collective-permute-done.11), channel_id=1, source_target_pairs={{0,1},{1,2},{2,3},{3,4},{4,5},{5,6},{6,7},{7,8},{8,9},{9,10},{10,1... | collective-permute-start | bytes 6152 | tf_op jit(solution)/shard_map/ppermute | solution.py:15
  85.1 5.7 %collective-permute-start.13 = (bf16[2,512]{1,0:T(2,128)(2,1)S(1)}, bf16[2,512]{1,0:T(2,128)(2,1)S(1)}, u32[]{:S(2)}, u32[]{:S(2)}) collective-permute-start(bf16[2,512]{1,0:T(2,128)(2,1)S(1)} %collective-permute-done.12), channel_id=1, source_target_pairs={{0,1},{1,2},{2,3},{3,4},{4,5},{5,6},{6,7},{7,8},{8,9},{9,10},{10,1... | collective-permute-start | bytes 6152 | tf_op jit(solution)/shard_map/ppermute | solution.py:15
  90.8 5.7 %collective-permute-start.14 = (bf16[2,512]{1,0:T(2,128)(2,1)S(1)}, bf16[2,512]{1,0:T(2,128)(2,1)S(1)}, u32[]{:S(2)}, u32[]{:S(2)}) collective-permute-start(bf16[2,512]{1,0:T(2,128)(2,1)S(1)} %collective-permute-done.13), channel_id=1, source_target_pairs={{0,1},{1,2},{2,3},{3,4},{4,5},{5,6},{6,7},{7,8},{8,9},{9,10},{10,1... | collective-permute-start | bytes 6152 | tf_op jit(solution)/shard_map/ppermute | solution.py:15
  105.0 61.2 %copy-start.5 = (bf16[2,2048]{1,0:T(2,128)(2,1)S(1)}, bf16[2,2048]{1,0:T(2,128)(2,1)}, u32[]{:S(2)}) copy-start(bf16[2,2048]{1,0:T(2,128)(2,1)} %param.8) | copy-start | bytes 24580
  306.8 5.4 %copy-start.3 = (f32[512,512]{1,0:T(8,128)S(1)}, f32[512,512]{1,0:T(8,128)}, u32[]{:S(2)}) copy-start(f32[512,512]{1,0:T(8,128)} %get-tuple-element.34) | copy-start | bytes 3145732
  (3 other events, 3.9 us)
Sparse Core Ops, SparseCore 0:
  169.3 137.4 all-reduce.4
